TPU v7x, 512 devices: a whole 4x4x16 slice. The times are simulated.
512 devices in a mesh: blk: 128 (over x, z, y_lo), frq: 4 (over y_hi, core).
Axes of the slice: x: 4, y: 4 (y_hi: 2, y_lo: 2; y = y_hi * 2 + y_lo), z: 16, core: 2. Of those that a mesh axis runs over, the one named last changes fastest.
Arguments:
- spectra: bfloat16 [2, 3, 2048, 512], P(None, None, 'blk', 'frq'), may hold values from -6 to 6
- observed: bfloat16 [32768, 3, 3, 1024], P(('blk', 'frq')), may hold values from -6 to 6
- own_station: int32 [128, 128, 2], P('blk'), may hold values from 0 to 15
- partner_station: int32 [128, 128, 2], P('blk'), may hold values from 0 to 15, as said below
- pair_count: int32 [128, 128], P('blk'), may hold values from 1 to 2, as said below
Outputs:
- adjoint: float32 [1024, 3, 2048], P('frq', None, 'blk')
Inputs may be any that keep to these rules, and one draw needn't show every extreme that they name: `partner_station`: within the reading block's own block pair, a slot's two stations differ. `pair_count`: the live slots of a block pair are its first ones; every reading block has a block pair with all 2 slots live.
All inputs are finite; a program needn't handle non-finite values.
Results may differ from a plain program's by a relative error of at most 0.003.
Values may be sent and summed in bfloat16 or wider, within the bound.
No kernel may reach another device: no remote copies, remote signals or barrier semaphores. Data moves between devices by JAX's collectives and lax.ppermute only.
A program may use at most 64 MiB of HBM per device.

v0:
```python
import math
import jax
import jax.numpy as jnp
from jax import lax
from jax.sharding import PartitionSpec as P

NF = 512
NT = 1024


def phase_table(freq_start, freq_count, time_count):
    freq_index = lax.iota(jnp.int32, freq_count) + freq_start
    time_index = lax.iota(jnp.int32, time_count)
    phase_num = (2 * freq_index + 1)[:, None] * time_index[None, :] % (2 * NT)
    return phase_num.astype(jnp.float32) * (math.pi / NT)


def lag_window():
    time_index = lax.iota(jnp.int32, NT)
    lag_size = jnp.minimum(time_index, NT - time_index)
    return ((lag_size >= NT // 32) & (lag_size < NT // 4)).astype(jnp.float32)


def cross_spectra(first_rows, second_rows):
    real_part = (
        first_rows[:, 0, :, None] * second_rows[:, 0, None, :]
        + first_rows[:, 1, :, None] * second_rows[:, 1, None, :]
    )
    imag_part = (
        first_rows[:, 1, :, None] * second_rows[:, 0, None, :]
        - first_rows[:, 0, :, None] * second_rows[:, 1, None, :]
    )
    return jnp.stack([real_part, imag_part], axis=3)


def pair_gradients(adjoint_rows, first_rows, second_rows):
    adj_real = adjoint_rows[:, :, :, 0]
    adj_imag = adjoint_rows[:, :, :, 1]
    own_real = jnp.sum(
        adj_real * second_rows[:, 0, None] - adj_imag * second_rows[:, 1, None], axis=2
    )
    own_imag = jnp.sum(
        adj_real * second_rows[:, 1, None] + adj_imag * second_rows[:, 0, None], axis=2
    )
    far_real = jnp.sum(
        adj_real * first_rows[:, 0, :, None] + adj_imag * first_rows[:, 1, :, None], axis=1
    )
    far_imag = jnp.sum(
        adj_real * first_rows[:, 1, :, None] - adj_imag * first_rows[:, 0, :, None], axis=1
    )
    return (jnp.stack([own_real, own_imag], axis=1), jnp.stack([far_real, far_imag], axis=1))


def local(spectra, observed, own_station, partner_station, pair_count):
    block_total = lax.axis_size("blk")
    band_total = lax.axis_size("frq")
    per_block = spectra.shape[2]
    freq_dev = spectra.shape[3]
    slot_cap = own_station.shape[2]
    slot_total = block_total * slot_cap
    item_count = slot_total // band_total
    band_index = lax.axis_index("frq")
    spec_rows = jnp.transpose(spectra, (2, 0, 1, 3))
    own_ids = own_station[0].reshape(slot_total)
    partner_local = partner_station[0]
    partner_ids = partner_local.reshape(slot_total)
    alive_mask = (
        (lax.iota(jnp.int32, slot_cap)[None, :] < pair_count[0][:, None])
        .reshape(slot_total)
        .astype(jnp.float32)
    )
    own_rows = jnp.take(spec_rows, own_ids, axis=0)
    part_rows = lax.all_gather(spec_rows, "blk", axis=0, tiled=True)
    first_row = jnp.int32(0)
    row_count = part_rows.shape[0]
    block_span = min(block_total, -(-row_count // per_block) + 1)
    first_block = jnp.clip(first_row // per_block, 0, block_total - block_span)
    slot_low = first_block * slot_cap
    slot_span = block_span * slot_cap
    block_of_slot = (slot_low + lax.iota(jnp.int32, slot_span)) // slot_cap
    global_ids = block_of_slot * per_block + partner_ids
    inside = (global_ids >= first_row) & (global_ids < first_row + row_count)
    fetched = jnp.take(part_rows, jnp.clip(global_ids, 0, row_count - 1), axis=0)
    fresh = (
        cross_spectra(own_rows.astype(jnp.float32), fetched.astype(jnp.float32))
        * alive_mask[:, None, None, None, None]
    ).astype(jnp.bfloat16)
    cross_old = jnp.zeros((slot_total, 3, 3, 2, freq_dev), jnp.bfloat16)
    rows_old = jnp.zeros((slot_total, 2, 3, freq_dev), jnp.bfloat16)
    cross_new = jnp.where(inside[:, None, None, None, None], fresh, cross_old)
    rows_new = jnp.where(inside[:, None, None, None], fetched, rows_old)
    phase = phase_table(0, NF, NT)
    basis = jnp.concatenate(
        [
            (jnp.cos(phase) / math.sqrt(NF)).astype(jnp.bfloat16),
            -(jnp.sin(phase) / math.sqrt(NF)).astype(jnp.bfloat16),
        ],
        axis=0,
    )
    window = lag_window()
    alive_band = lax.dynamic_slice_in_dim(alive_mask, band_index * item_count, item_count)
    observed_rows = observed.reshape(item_count * 9, NT).astype(jnp.float32)
    station_iota = lax.iota(jnp.int32, per_block)
    sent = cross_new.reshape(band_total, item_count, 3, 3, 2, freq_dev)
    whole_band = lax.all_to_all(sent, "frq", split_axis=0, concat_axis=5, tiled=True)
    correlation = jnp.dot(
        whole_band.reshape(item_count * 9, 2 * NF), basis, preferred_element_type=jnp.float32
    )
    residual = (
        (correlation - observed_rows) * jnp.repeat(alive_band, 9)[:, None] * window[None, :]
    ).astype(jnp.bfloat16)
    adjoint_rows = (
        lax.dot_general(
            residual, basis, (((1,), (1,)), ((), ())), preferred_element_type=jnp.float32
        )
        .astype(jnp.bfloat16)
        .reshape(1, item_count, 3, 3, 2, NF)
    )
    returned = lax.all_to_all(adjoint_rows, "frq", split_axis=5, concat_axis=0, tiled=True).reshape(
        slot_total, 3, 3, 2, freq_dev
    )
    own_grad, far_grad = pair_gradients(
        returned.astype(jnp.float32), own_rows.astype(jnp.float32), rows_new.astype(jnp.float32)
    )
    own_onehot = (own_ids[None, :] == station_iota[:, None]).astype(jnp.float32)
    grad_local = jnp.dot(
        own_onehot,
        own_grad.reshape(slot_total, 6 * freq_dev),
        precision=lax.Precision.HIGHEST,
        preferred_element_type=jnp.float32,
    )
    far_block = far_grad.reshape(block_total, slot_cap, 2, 3, freq_dev)
    back_grad, back_ids = (
        lax.all_to_all(
            far_block.astype(jnp.bfloat16), "blk", split_axis=0, concat_axis=0, tiled=True
        ).astype(far_block.dtype),
        lax.all_to_all(partner_local, "blk", split_axis=0, concat_axis=0, tiled=True),
    )
    back_onehot = (back_ids.reshape(slot_total)[None, :] == station_iota[:, None]).astype(
        jnp.float32
    )
    station_grad = grad_local + jnp.dot(
        back_onehot,
        back_grad.reshape(slot_total, 6 * freq_dev),
        precision=lax.Precision.HIGHEST,
        preferred_element_type=jnp.float32,
    )
    grad_matrix = jnp.transpose(
        station_grad.reshape(per_block, 2, 3, freq_dev), (1, 3, 2, 0)
    ).reshape(2 * freq_dev, 3 * per_block)
    output_scale = 1.0 / math.sqrt(2.0 * block_total * slot_cap / per_block)
    phase_part = phase_table(
        band_index * freq_dev, freq_dev, NT // band_total * lax.axis_size("frq")
    )
    basis_part = jnp.concatenate(
        [jnp.cos(phase_part) / math.sqrt(NF), -(jnp.sin(phase_part) / math.sqrt(NF))], axis=0
    )
    product = lax.dot_general(
        basis_part,
        grad_matrix,
        (((0,), (0,)), ((), ())),
        precision=lax.Precision.HIGHEST,
        preferred_element_type=jnp.float32,
    )
    return lax.psum_scatter(
        product.reshape(NT // band_total * lax.axis_size("frq"), 3, per_block) * output_scale,
        "frq",
        scatter_dimension=0,
        tiled=True,
    )


def solution(mesh):
    return jax.shard_map(
        local,
        mesh=mesh,
        in_specs=(
            P(None, None, "blk", "frq"),
            P(("blk", "frq"), None, None, None),
            P("blk", None, None),
            P("blk", None, None),
            P("blk", None),
        ),
        out_specs=P("frq", None, "blk"),
        check_vma=False,
    )
```

profile of v0, /device:TPU:1, one launch (start us, length us, event | category | flops | bytes accessed | tf_op | source)
XLA Modules:
  0.0 784.7 jit_solution(10995173478806446138)
XLA Ops:
  6.5 1.4 copy.169
  7.9 1.4 copy.126
  9.3 1.0 reshape_squeeze.13
  10.3 1.0 reshape_squeeze.12
  11.3 0.8 copy.125
  12.1 0.1 reshape_squeeze.11
  12.2 0.1 eq.34
  12.4 0.9 reshape_squeeze.10
  13.3 2.2 gather_fusion
  15.6 1.0 fusion.16
  16.6 0.6 fusion.40
  17.2 1.0 copy_bitcast_fusion.4
  18.3 1.1 copy.130
  19.3 1.1 copy.136
  20.4 0.5 broadcast.383
  20.9 0.6 reduce.6
  22.3 0.1 mul.323
  22.4 2.3 copy.142
  24.7 2.6 reshape.280
  27.4 493.7 %all-gather.2.cloned.1.call-done = bf16[2048,2,3,128]{3,1,2,0:T(2,128)(2,1)} async-done(((bf16[16,2,3,128]{3,1,2,0:T(2,128)(2,1)}), bf16[2048,2,3,128]{3,1,2,0:T(2,128)(2,1)}) %all-gather.2.cloned.1.call-update) | async-done | bytes 3145744 | tf_op jit(solution)/shard_map/all_gather | solution.py:73
  521.1 3.4 gather_fusion.1
  524.5 1.5 fusion.17
  525.9 2.1 fusion.39
  528.1 0.3 copy.134
  528.4 0.3 copy.138
  528.7 0.4 copy-done
  529.1 0.2 copy-done.1
  529.2 2.5 multiply_add_fusion
  531.7 3.6 broadcast_select_fusion
  535.3 91.7 %all-to-all-start = ((bf16[4,64,3,3,2,128]{5,4,3,2,1,0:T(2,128)(2,1)}), bf16[4,64,3,3,2,128]{5,4,3,2,1,0:T(2,128)(2,1)S(1)}, u32[]{:S(2)}, u32[]{:S(2)}) async-start(bf16[4,64,3,3,2,128]{5,4,3,2,1,0:T(2,128)(2,1)} %broadcast_select_fusion), calls=%async_computation | async-start | bytes 2359296 | tf_op jit(solution)/shard_map/all_to_all | solution.py:105
  626.9 8.4 %multiply_convert_fusion.2 = bf16[512,1024]{1,0:T(8,128)(2,1)S(1)} fusion(s32[512]{0:T(512)S(1)} %multiply_add_fusion.1), kind=kLoop, calls=%fused_computation.14 | loop fusion | flops 8388608 | bytes 1050624 | tf_op jit(solution)/shard_map/convert_element_type | solution.py:95
  635.3 9.1 %fusion.7 = bf16[512,1024]{1,0:T(8,128)(2,1)} fusion(s32[512]{0:T(512)S(1)} %multiply_add_fusion.1), kind=kLoop, calls=%fused_computation.29 | loop fusion | flops 9961472 | bytes 1050624 | tf_op jit(solution)/shard_map/neg | solution.py:96
  644.5 1.5 copy.141
  646.0 0.9 reshape.274
  646.8 4.9 convolution_convert_fusion
  651.7 0.9 reshape.275
  652.6 3.6 copy.143
  656.2 2.9 reshape.317
  659.1 4.9 all-to-all-start.1
  664.0 0.8 copy.166
  664.8 0.8 copy.167
  665.6 14.9 %all-to-all-done.1 = bf16[4,2,73728]{2,1,0:T(2,128)(2,1)S(1)} async-done(((bf16[4,2,73728]{2,1,0:T(2,128)(2,1)}), bf16[4,2,73728]{2,1,0:T(2,128)(2,1)S(1)}, u32[]{:S(2)}, u32[]{:S(2)}) %all-to-all-start.1) | async-done | bytes 1179680 | tf_op jit(solution)/shard_map/all_to_all | solution.py:119
  680.5 7.7 all-to-all-start.2
  688.3 1.6 reshape.318
  689.8 3.1 copy.144
  693.0 1.8 copy.145
  694.8 0.4 copy.146
  695.2 0.5 copy-done.2
  696.1 0.7 subtract_reduce_fusion.1
  696.8 0.3 copy.153
  697.1 0.3 copy.154
  697.5 1.6 pad_maximum_fusion.6
  699.1 2.9 all-to-all-done.2
  702.0 13.4 %all-to-all-start.3 = ((bf16[128,2,2,3,128]{4,2,3,1,0:T(2,128)(2,1)}), bf16[128,2,2,3,128]{4,2,3,1,0:T(2,128)(2,1)S(1)}, u32[]{:S(2)}, u32[]{:S(2)}) async-start(bf16[128,2,2,3,128]{4,2,3,1,0:T(2,128)(2,1)} %pad_maximum_fusion.6), calls=%async_computation.3 | async-start | bytes 786432 | tf_op jit(solution)/shard_map/all_to_all | solution.py:134
  715.4 2.1 cosine_multiply_fusion
  717.6 1.6 reduce.7
  719.3 0.3 copy.149
  719.6 21.0 %all-to-all-done.3 = bf16[128,2,2,3,128]{4,2,3,1,0:T(2,128)(2,1)S(1)} async-done(((bf16[128,2,2,3,128]{4,2,3,1,0:T(2,128)(2,1)}), bf16[128,2,2,3,128]{4,2,3,1,0:T(2,128)(2,1)S(1)}, u32[]{:S(2)}, u32[]{:S(2)}) %all-to-all-start.3) | async-done | bytes 393248 | tf_op jit(solution)/shard_map/all_to_all | solution.py:134
  740.6 0.2 copy.155
  740.8 0.3 reshape.277
  741.2 0.2 fusion.19
  741.3 0.5 convolution_add_fusion
  741.9 1.5 convolution_multiply_fusion
  743.4 34.5 %reduce-scatter.2.cloned.1.call-done = f32[256,3,16]{0,2,1:T(8,128)} async-done(((f32[1024,3,16]{0,2,1:T(8,128)}), f32[256,3,16]{0,2,1:T(8,128)}) %reduce-scatter.2.cloned.1.call-update) | async-done | bytes 49168 | tf_op jit(solution)/shard_map/reduce_scatter | solution.py:165
  (49 shorter events, 1.6 us)
Async XLA Ops:
  6.5 514.5 %all-gather.2.cloned.1.call-start = ((), (), s32[]{:S(2)}) async-start(), calls=%async_computation.5 | async-start | bytes 3170304 | tf_op jit(solution)/shard_map/all_gather | solution.py:73
  17.2 3.7 copy-start.8
  528.0 1.0 copy-start
  528.0 1.2 copy-start.1
  535.3 109.2 %all-to-all-start = ((bf16[4,64,3,3,2,128]{5,4,3,2,1,0:T(2,128)(2,1)}), bf16[4,64,3,3,2,128]{5,4,3,2,1,0:T(2,128)(2,1)S(1)}, u32[]{:S(2)}, u32[]{:S(2)}) async-start(bf16[4,64,3,3,2,128]{5,4,3,2,1,0:T(2,128)(2,1)} %broadcast_select_fusion), calls=%async_computation | async-start | bytes 2359296 | tf_op jit(solution)/shard_map/all_to_all | solution.py:105
  656.2 7.8 copy-start.5
  659.1 5.7 copy-start.4
  659.1 21.4 %all-to-all-start.1 = ((bf16[4,2,73728]{2,1,0:T(2,128)(2,1)}), bf16[4,2,73728]{2,1,0:T(2,128)(2,1)S(1)}, u32[]{:S(2)}, u32[]{:S(2)}) async-start(bf16[4,2,73728]{2,1,0:T(2,128)(2,1)} %reshape.317), calls=%async_computation.1 | async-start | bytes 2359296 | tf_op jit(solution)/shard_map/all_to_all | solution.py:119
  680.5 21.4 %all-to-all-start.2 = ((s32[128,1,2]{2,1,0:T(1,128)}), s32[128,1,2]{2,1,0:T(1,128)}, u32[]{:S(2)}, u32[]{:S(2)}) async-start(s32[128,1,2]{2,1,0:T(1,128)} %bitcast.22), calls=%async_computation.2 | async-start | bytes 131072 | tf_op jit(solution)/shard_map/all_to_all | solution.py:137
  694.8 1.0 copy-start.2
  694.8 1.1 copy-start.3
  694.8 1.2 copy-start.6
  694.8 1.3 copy-start.7
  702.0 38.7 %all-to-all-start.3 = ((bf16[128,2,2,3,128]{4,2,3,1,0:T(2,128)(2,1)}), bf16[128,2,2,3,128]{4,2,3,1,0:T(2,128)(2,1)S(1)}, u32[]{:S(2)}, u32[]{:S(2)}) async-start(bf16[128,2,2,3,128]{4,2,3,1,0:T(2,128)(2,1)} %pad_maximum_fusion.6), calls=%async_computation.3 | async-start | bytes 786432 | tf_op jit(solution)/shard_map/all_to_all | solution.py:134
  715.4 62.5 %reduce-scatter.2.cloned.1.call-start = ((), (), s32[]{:S(2)}) async-start(), calls=%async_computation.6 | async-start | bytes 245760 | tf_op jit(solution)/shard_map/reduce_scatter | solution.py:165
Sparse Core Ops, SparseCore 0:
  9.4 511.5 all-gather.1
  743.5 34.2 reduce-scatter.1
where the time goes:
time: 786 us; the launch traced here: 785 us
  waiting for transfers between devices  567 us (72%)
  starting transfers between devices  118 us (15%)
  local copies, waits for them, and re-layouts  46.3 us (6%)
  other arithmetic  32.8 us (4%)
  between operations  13.8 us (2%)
    all_gather x1, waiting for transfers between devices, local(): part_rows = lax.all_gather(spec_rows, 'blk', axis=0, tiled=True)  494 us
    all_to_all x1, starting transfers between devices, local(): lax.all_to_all(sent, 'frq', split_axis=0, concat_axis=5, tiled=True)  91.7 us
    reduce_scatter x1, waiting for transfers between devices, local(): lax.psum_scatter(product.reshape(NT // band_total * lax.axis_size('frq'),...  34.5 us
    all_to_all x1, waiting for transfers between devices, local(): lax.all_to_all(far_block.astype(jnp.bfloat16), 'blk', split_axis=0, conca...  21 us
  transfers between devices with their start and end apart: 6, of which 5 were waited for; matrix products, arithmetic and copies ran while one was open for 7% of the time, Pallas kernels for 0%

commit v1 on v0

--- a/solution.py
+++ b/solution.py
@@ -70,7 +70,9 @@
         .astype(jnp.float32)
     )
     own_rows = jnp.take(spec_rows, own_ids, axis=0)
-    part_rows = lax.all_gather(spec_rows, "blk", axis=0, tiled=True)
+    part_rows = jnp.concatenate(
+        lax.all_to_all(jnp.stack([spec_rows] * lax.axis_size("blk")), "blk", 0, 0), axis=0
+    )
     first_row = jnp.int32(0)
     row_count = part_rows.shape[0]
     block_span = min(block_total, -(-row_count // per_block) + 1)

time: 786 us -> 360 us (0.46)
  waiting for transfers between devices: 567 us -> 195 us
  starting transfers between devices: 118 us -> 58.9 us
    all_gather x1 -> x0, waiting for transfers between devices: 494 us -> none  [local(): part_rows = lax.all_gather(spec_rows, 'blk', axis=0, tiled=True)]
    all_to_all x0 -> x1, waiting for transfers between devices: none -> 122 us  [local(): lax.all_to_all(jnp.stack([spec_rows] * lax.axis_size('blk')), 'blk', 0, 0)]
    all_to_all x1, starting transfers between devices: 91.7 us -> 10 us  [local(): lax.all_to_all(sent, 'frq', split_axis=0, concat_axis=5, tiled=True)]
    all_to_all x0 -> x1, starting transfers between devices: none -> 22.4 us  [local(): lax.all_to_all(jnp.stack([spec_rows] * lax.axis_size('blk')), 'blk', 0, 0)]
  transfers between devices with their start and end apart: 6 -> 6, of which waited for: 5 -> 5; matrix products, arithmetic and copies ran while one was open for 7% -> 14% of each run, Pallas kernels for 0% -> 0%
where the time goes in v1:
time: 360 us; the launch traced here: 356 us
  waiting for transfers between devices  195 us (54%)
  starting transfers between devices  58.9 us (16%)
  local copies, waits for them, and re-layouts  47 us (13%)
  other arithmetic  33 us (9%)
  between operations  14.1 us (4%)
  matrix products  7 us (2%)
    all_to_all x1, waiting for transfers between devices, local(): lax.all_to_all(jnp.stack([spec_rows] * lax.axis_size('blk')), 'blk', 0, 0)  122 us
    reduce_scatter x1, waiting for transfers between devices, local(): lax.psum_scatter(product.reshape(NT // band_total * lax.axis_size('frq'),...  34.5 us
    all_to_all x1, starting transfers between devices, local(): lax.all_to_all(jnp.stack([spec_rows] * lax.axis_size('blk')), 'blk', 0, 0)  22.4 us
    all_to_all x1, waiting for transfers between devices, local(): lax.all_to_all(far_block.astype(jnp.bfloat16), 'blk', split_axis=0, conca...  20.9 us
    all_to_all x1, waiting for transfers between devices, local(): lax.all_to_all(adjoint_rows, 'frq', split_axis=5, concat_axis=0, tiled=True)  14.9 us
    all_to_all x1, starting transfers between devices, local(): lax.all_to_all(far_block.astype(jnp.bfloat16), 'blk', split_axis=0, conca...  13.5 us
    all_to_all x1, starting transfers between devices, local(): lax.all_to_all(sent, 'frq', split_axis=0, concat_axis=5, tiled=True)  10 us
    neg x1, other arithmetic, local(): -(jnp.sin(phase) / math.sqrt(NF)).astype(jnp.bfloat16)  9.12 us
  transfers between devices with their start and end apart: 6, of which 5 were waited for; matrix products, arithmetic and copies ran while one was open for 14% of the time, Pallas kernels for 0%

profile of v1, /device:TPU:1, one launch (start us, length us, event | category | flops | bytes accessed | tf_op | source)
XLA Modules:
  0.0 355.5 jit_solution(6561156362725563043)
XLA Ops:
  6.5 0.8 copy.170
  7.3 3.3 stack.16
  10.6 22.4 %all-to-all-start = ((bf16[128,16,2,3,128]{4,2,3,1,0:T(2,128)(2,1)}), bf16[128,16,2,3,128]{4,2,3,1,0:T(2,128)(2,1)}, u32[]{:S(2)}, u32[]{:S(2)}) async-start(bf16[128,16,2,3,128]{4,2,3,1,0:T(2,128)(2,1)} %stack.16), calls=%async_computation | async-start | bytes 6291456 | tf_op jit(solution)/shard_map/all_to_all | solution.py:74
  33.0 0.7 copy.127
  33.7 1.0 reshape_squeeze.13
  34.7 1.0 reshape_squeeze.12
  36.0 0.1 eq.34
  36.1 0.9 reshape_squeeze.10
  37.1 1.5 gather_fusion
  38.6 1.0 fusion.16
  39.6 0.6 fusion.40
  40.3 1.0 copy_bitcast_fusion.4
  41.3 1.1 copy.131
  42.3 1.1 copy.137
  43.5 0.5 broadcast.385
  44.0 0.7 reduce.6
  45.4 0.1 mul.323
  45.6 2.3 copy.143
  47.9 2.6 reshape.286
  50.6 122.0 %all-to-all-done = bf16[128,16,2,3,128]{4,2,3,1,0:T(2,128)(2,1)} async-done(((bf16[128,16,2,3,128]{4,2,3,1,0:T(2,128)(2,1)}), bf16[128,16,2,3,128]{4,2,3,1,0:T(2,128)(2,1)}, u32[]{:S(2)}, u32[]{:S(2)}) %all-to-all-start) | async-done | bytes 3145760 | tf_op jit(solution)/shard_map/all_to_all | solution.py:74
  172.6 3.4 gather_fusion.1
  176.0 1.5 fusion.17
  177.5 2.1 fusion.39
  179.6 0.3 copy.135
  180.0 0.3 copy.139
  180.2 0.4 copy-done
  180.6 0.2 copy-done.1
  180.8 2.5 multiply_add_fusion
  183.3 3.6 %broadcast_select_fusion = bf16[4,64,3,3,2,128]{5,4,3,2,1,0:T(2,128)(2,1)} fusion(pred[4,64]{1,0:T(4,128)(4,1)S(1)} %compare_and_fusion.3, f32[4,64]{1,0:T(4,128)S(1)} %compare_convert_fusion, f32[4,64,3,3,1,128]{5,4,3,2,1,0:T(1,128)S(1)} %get-tuple-element.14, f32[4,64,3,3,1,128]{5,4,3,2,1,0:T(1,128)S(1)} %get-tuple-element.13), kind=kLoop, calls=%fused_computation.8 | loop fusion | flops 2359296 | bytes 3540224 | tf_op jit(solution)/shard_map/jit(_where)/select_n | solution.py:92
  186.8 10.0 %all-to-all-start.1 = ((bf16[4,64,3,3,2,128]{5,4,3,2,1,0:T(2,128)(2,1)}), bf16[4,64,3,3,2,128]{5,4,3,2,1,0:T(2,128)(2,1)S(1)}, u32[]{:S(2)}, u32[]{:S(2)}) async-start(bf16[4,64,3,3,2,128]{5,4,3,2,1,0:T(2,128)(2,1)} %broadcast_select_fusion), calls=%async_computation.1 | async-start | bytes 2359296 | tf_op jit(solution)/shard_map/all_to_all | solution.py:107
  196.9 8.4 %multiply_convert_fusion.2 = bf16[512,1024]{1,0:T(8,128)(2,1)S(1)} fusion(s32[512]{0:T(512)S(1)} %multiply_add_fusion.1), kind=kLoop, calls=%fused_computation.14 | loop fusion | flops 8388608 | bytes 1050624 | tf_op jit(solution)/shard_map/convert_element_type | solution.py:97
  205.3 9.1 %fusion.7 = bf16[512,1024]{1,0:T(8,128)(2,1)} fusion(s32[512]{0:T(512)S(1)} %multiply_add_fusion.1), kind=kLoop, calls=%fused_computation.29 | loop fusion | flops 9961472 | bytes 1050624 | tf_op jit(solution)/shard_map/neg | solution.py:98
  214.4 1.5 copy.142
  215.9 0.9 reshape.280
  216.8 4.9 %convolution_convert_fusion = bf16[576,1024]{1,0:T(8,128)(2,1)S(1)} fusion(bf16[512,1024]{1,0:T(8,128)(2,1)} %fusion.7, bf16[512,1024]{1,0:T(8,128)(2,1)S(1)} %multiply_convert_fusion.2, f32[576,1024]{1,0:T(8,128)} %reshape.286, bf16[576,1024]{1,0:T(8,128)(2,1)S(1)} %reshape.280, f32[1024]{0:T(1024)S(1)} %fusion.25, f32[576]{0:T(1024)S(1)} %mul.323), kind=kOutput, calls=%fused_computation.18 | convolution fusion | flops 2427256832 | bytes 6822144 | tf_op jit(solution)/shard_map/dot_general | solution.py:115
  221.7 0.9 reshape.281
  222.6 3.6 %copy.144 = bf16[1,64,3,3,2,512]{1,4,3,2,0,5:T(2,128)(2,1)S(1)} copy(bf16[1,64,3,3,2,512]{5,4,3,2,1,0:T(2,128)(2,1)S(1)} %reshape.281) | data formatting | bytes 2359296 | tf_op jit(solution)/shard_map/reshape | solution.py:119
  226.2 2.9 reshape.323
  229.0 4.9 %all-to-all-start.2 = ((bf16[4,2,73728]{2,1,0:T(2,128)(2,1)}), bf16[4,2,73728]{2,1,0:T(2,128)(2,1)S(1)}, u32[]{:S(2)}, u32[]{:S(2)}) async-start(bf16[4,2,73728]{2,1,0:T(2,128)(2,1)} %reshape.323), calls=%async_computation.2 | async-start | bytes 2359296 | tf_op jit(solution)/shard_map/all_to_all | solution.py:121
  234.0 0.8 copy.167
  234.8 0.8 copy.168
  235.5 14.9 %all-to-all-done.2 = bf16[4,2,73728]{2,1,0:T(2,128)(2,1)S(1)} async-done(((bf16[4,2,73728]{2,1,0:T(2,128)(2,1)}), bf16[4,2,73728]{2,1,0:T(2,128)(2,1)S(1)}, u32[]{:S(2)}, u32[]{:S(2)}) %all-to-all-start.2) | async-done | bytes 1179680 | tf_op jit(solution)/shard_map/all_to_all | solution.py:121
  250.5 8.0 %all-to-all-start.3 = ((s32[128,1,2]{2,1,0:T(1,128)}), s32[128,1,2]{2,1,0:T(1,128)}, u32[]{:S(2)}, u32[]{:S(2)}) async-start(s32[128,1,2]{2,1,0:T(1,128)} %bitcast.23), calls=%async_computation.3 | async-start | bytes 131072 | tf_op jit(solution)/shard_map/all_to_all | solution.py:139
  258.5 1.6 reshape.324
  260.0 3.1 copy.145
  263.1 1.8 copy.146
  265.0 0.4 copy.147
  265.4 0.5 copy-done.2
  266.3 0.7 subtract_reduce_fusion.1
  267.0 0.3 copy.154
  267.3 0.3 copy.155
  267.6 1.6 pad_maximum_fusion.6
  269.3 3.1 all-to-all-done.3
  272.4 13.5 %all-to-all-start.4 = ((bf16[128,2,2,3,128]{4,2,3,1,0:T(2,128)(2,1)}), bf16[128,2,2,3,128]{4,2,3,1,0:T(2,128)(2,1)S(1)}, u32[]{:S(2)}, u32[]{:S(2)}) async-start(bf16[128,2,2,3,128]{4,2,3,1,0:T(2,128)(2,1)} %pad_maximum_fusion.6), calls=%async_computation.4 | async-start | bytes 786432 | tf_op jit(solution)/shard_map/all_to_all | solution.py:136
  286.0 2.1 cosine_multiply_fusion
  288.2 1.7 reduce.7
  290.0 0.3 copy.150
  290.3 20.9 %all-to-all-done.4 = bf16[128,2,2,3,128]{4,2,3,1,0:T(2,128)(2,1)S(1)} async-done(((bf16[128,2,2,3,128]{4,2,3,1,0:T(2,128)(2,1)}), bf16[128,2,2,3,128]{4,2,3,1,0:T(2,128)(2,1)S(1)}, u32[]{:S(2)}, u32[]{:S(2)}) %all-to-all-start.4) | async-done | bytes 393248 | tf_op jit(solution)/shard_map/all_to_all | solution.py:136
  311.2 0.2 copy.156
  311.4 0.3 reshape.283
  311.7 0.2 fusion.19
  311.9 0.5 convolution_add_fusion
  312.5 1.5 convolution_multiply_fusion
  314.0 34.5 %reduce-scatter.2.cloned.1.call-done = f32[256,3,16]{0,2,1:T(8,128)} async-done(((f32[1024,3,16]{0,2,1:T(8,128)}), f32[256,3,16]{0,2,1:T(8,128)}) %reduce-scatter.2.cloned.1.call-update) | async-done | bytes 49168 | tf_op jit(solution)/shard_map/reduce_scatter | solution.py:167
  (53 shorter events, 1.9 us)
Async XLA Ops:
  10.6 22.4 %copy-start.8 = (s32[1,128,2]{1,2,0:T(2,128)S(1)}, s32[1,128,2]{1,2,0:T(2,128)}, u32[]{:S(2)}) copy-start(s32[1,128,2]{1,2,0:T(2,128)} %param.8) | copy-start | bytes 3076
  10.6 25.1 %copy-start.9 = (s32[1,128,2]{1,2,0:T(2,128)S(1)}, s32[1,128,2]{1,2,0:T(2,128)}, u32[]{:S(2)}) copy-start(s32[1,128,2]{1,2,0:T(2,128)} %param.7) | copy-start | bytes 3076
  10.6 162.0 %all-to-all-start = ((bf16[128,16,2,3,128]{4,2,3,1,0:T(2,128)(2,1)}), bf16[128,16,2,3,128]{4,2,3,1,0:T(2,128)(2,1)}, u32[]{:S(2)}, u32[]{:S(2)}) async-start(bf16[128,16,2,3,128]{4,2,3,1,0:T(2,128)(2,1)} %stack.16), calls=%async_computation | async-start | bytes 6291456 | tf_op jit(solution)/shard_map/all_to_all | solution.py:74
  40.2 3.7 %copy-start.10 = (s32[1,128]{1,0:T(1,128)S(1)}, s32[1,128]{1,0:T(1,128)}, u32[]{:S(2)}) copy-start(s32[1,128]{1,0:T(1,128)} %param.9) | copy-start | bytes 1540
  179.6 1.0 copy-start
  179.6 1.2 copy-start.1
  186.8 27.6 %all-to-all-start.1 = ((bf16[4,64,3,3,2,128]{5,4,3,2,1,0:T(2,128)(2,1)}), bf16[4,64,3,3,2,128]{5,4,3,2,1,0:T(2,128)(2,1)S(1)}, u32[]{:S(2)}, u32[]{:S(2)}) async-start(bf16[4,64,3,3,2,128]{5,4,3,2,1,0:T(2,128)(2,1)} %broadcast_select_fusion), calls=%async_computation.1 | async-start | bytes 2359296 | tf_op jit(solution)/shard_map/all_to_all | solution.py:107
  226.2 7.8 %copy-start.5 = (f32[256,1,3,128]{3,1,2,0:T(1,128)S(1)}, f32[256,1,3,128]{3,1,2,0:T(1,128)}, u32[]{:S(2)}) copy-start(f32[256,1,3,128]{3,1,2,0:T(1,128)} %get-tuple-element.16) | copy-start | bytes 1179652
  229.0 5.7 %copy-start.4 = (f32[256,1,3,128]{3,1,2,0:T(1,128)S(1)}, f32[256,1,3,128]{3,1,2,0:T(1,128)}, u32[]{:S(2)}) copy-start(f32[256,1,3,128]{3,1,2,0:T(1,128)} %get-tuple-element.15) | copy-start | bytes 1179652
  229.0 21.4 %all-to-all-start.2 = ((bf16[4,2,73728]{2,1,0:T(2,128)(2,1)}), bf16[4,2,73728]{2,1,0:T(2,128)(2,1)S(1)}, u32[]{:S(2)}, u32[]{:S(2)}) async-start(bf16[4,2,73728]{2,1,0:T(2,128)(2,1)} %reshape.323), calls=%async_computation.2 | async-start | bytes 2359296 | tf_op jit(solution)/shard_map/all_to_all | solution.py:121
  250.5 21.9 %all-to-all-start.3 = ((s32[128,1,2]{2,1,0:T(1,128)}), s32[128,1,2]{2,1,0:T(1,128)}, u32[]{:S(2)}, u32[]{:S(2)}) async-start(s32[128,1,2]{2,1,0:T(1,128)} %bitcast.23), calls=%async_computation.3 | async-start | bytes 131072 | tf_op jit(solution)/shard_map/all_to_all | solution.py:139
  265.0 1.0 copy-start.2
  265.0 1.1 copy-start.3
  265.0 1.2 copy-start.6
  265.0 1.3 copy-start.7
  272.4 38.8 %all-to-all-start.4 = ((bf16[128,2,2,3,128]{4,2,3,1,0:T(2,128)(2,1)}), bf16[128,2,2,3,128]{4,2,3,1,0:T(2,128)(2,1)S(1)}, u32[]{:S(2)}, u32[]{:S(2)}) async-start(bf16[128,2,2,3,128]{4,2,3,1,0:T(2,128)(2,1)} %pad_maximum_fusion.6), calls=%async_computation.4 | async-start | bytes 786432 | tf_op jit(solution)/shard_map/all_to_all | solution.py:136
  285.9 62.5 %reduce-scatter.2.cloned.1.call-start = ((), (), s32[]{:S(2)}) async-start(), calls=%async_computation.6 | async-start | bytes 245760 | tf_op jit(solution)/shard_map/reduce_scatter | solution.py:167
Sparse Core Ops, SparseCore 0:
  314.1 34.2 reduce-scatter.1
